TPU v7x, 32 devices: a whole 2x2x4 slice. The times are simulated.
32 devices in a mesh: group: 4 (over z), member: 8 (over y, x, core).
Axes of the slice: x: 2, y: 2, z: 4, core: 2. Of those that a mesh axis runs over, the one named last changes fastest.
Arguments:
- query_feat: bfloat16 [4096, 4096], P(('group', 'member'))
- code_feat: bfloat16 [4096, 4096], P(('group', 'member'))
- projection: bfloat16 [4096, 1024], replicated
- hard_ids: int32 [32, 16], P(('group', 'member')), may hold values from 0 to 63, as said below
- loss_weight: float32 [4096], P(('group', 'member')), may hold values from 1 to 4
Outputs:
- query_grad: bfloat16 [4096, 4096], P(('group', 'member'))
- code_grad: bfloat16 [4096, 4096], P(('group', 'member'))
- projection_grad: float32 [4096, 1024], P(('group', 'member'))
Inputs may be any that keep to these rules, and one draw needn't show every extreme that they name: `hard_ids`: entry (owner device g * 8 + m) * 2 + slot names code rows of that device. A row names 16 different blocks, none of its own group; at most 8 of them lie in one group, and exactly 8 in some group of every row.
All inputs are finite; a program needn't handle non-finite values.
Results may differ from a plain program's by a relative error of at most 0.02.
Values may be sent and summed in bfloat16 or wider, within the bound.
No kernel may reach another device: no remote copies, remote signals or barrier semaphores. Data moves between devices by JAX's collectives and lax.ppermute only.
A program may use at most 128 MiB of HBM per device.

v0:
```python
import jax
import jax.numpy as jnp
from jax import lax
from jax.sharding import PartitionSpec as P

CB = 64
inverse_temp = 120.0
epsilon = 1e-06


def embed(features, projection):
    values = jnp.dot(features, projection, preferred_element_type=jnp.float32)
    inverse = lax.rsqrt(jnp.sum(values * values, axis=1) + epsilon)
    unit_vec = values * inverse[:, None]
    return (unit_vec, inverse, unit_vec.astype(jnp.bfloat16))


def norm_back(upstream, unit_vec, inverse):
    inner_prod = jnp.sum(unit_vec * upstream, axis=1, keepdims=True)
    return (inverse[:, None] * (upstream - unit_vec * inner_prod)).astype(jnp.bfloat16)


def body(query_feat, code_feat, projection, hard_ids, loss_weight):
    groups = lax.axis_size("group")
    members = lax.axis_size("member")
    group_index = lax.axis_index("group")
    member_index = lax.axis_index("member")
    queries_dev = query_feat.shape[0]
    feat_width = query_feat.shape[1]
    emb_width = projection.shape[1]
    slot_count = queries_dev // CB
    per_group = members * slot_count
    group_span = members * queries_dev
    rows_dev = feat_width // (groups * members)
    feats = jnp.stack([query_feat, code_feat], axis=0).reshape(
        2, queries_dev, groups, members, rows_dev
    )
    feats = jnp.transpose(feats, (3, 0, 1, 2, 4))
    feat_cols = lax.all_to_all(feats, "member", split_axis=0, concat_axis=0, tiled=True)
    q_unit, q_inv, q_emb = embed(query_feat, projection)
    c_unit, c_inv, c_emb = embed(code_feat, projection)
    group_codes = lax.all_gather(c_emb, "member", axis=0, tiled=True)
    q_all = lax.all_gather(q_emb, "group", axis=0)
    ids_all = lax.all_gather(hard_ids[0], "group", axis=0)
    w_all = lax.all_gather(loss_weight, "group", axis=0)
    block_ids = group_index * per_group + jnp.arange(per_group, dtype=jnp.int32)
    asked = jnp.any(ids_all[:, :, None] == block_ids[None, None, :], axis=1)
    own = jnp.arange(groups, dtype=jnp.int32) == group_index
    block_mask = asked | own[:, None]
    col_mask = jnp.broadcast_to(block_mask[:, :, None], (groups, per_group, CB)).reshape(
        groups, 1, group_span
    )
    scores = inverse_temp * jnp.einsum(
        "gqe,ke->gqk", q_all, group_codes, preferred_element_type=jnp.float32
    )
    scores = jnp.where(col_mask, scores, -jnp.inf)
    part_max = jnp.max(scores, axis=2)
    safe_max = jnp.where(part_max > -jnp.inf, part_max, 0.0)
    part_sum = jnp.sum(jnp.exp(scores - safe_max[:, :, None]), axis=2)
    stats = lax.all_gather(jnp.stack([part_max, part_sum], axis=0), "group", axis=0)
    row_max = jnp.max(stats[:, 0], axis=0)
    row_sum = jnp.sum(stats[:, 1] * jnp.exp(stats[:, 0] - row_max[None]), axis=0)
    log_total = row_max + jnp.log(row_sum)
    offsets = jnp.arange(queries_dev, dtype=jnp.int32)
    columns = jnp.arange(group_span, dtype=jnp.int32)
    positive = (columns[None, :] == (member_index * queries_dev + offsets)[:, None]).astype(
        jnp.float32
    )
    positive = positive[None] * own[:, None, None].astype(jnp.float32)
    factor = w_all * inverse_temp
    grad = (factor[:, :, None] * (jnp.exp(scores - log_total[:, :, None]) - positive)).astype(
        jnp.bfloat16
    )
    delta_parts = jnp.einsum("gqk,ke->gqe", grad, group_codes, preferred_element_type=jnp.float32)
    query_delta = lax.psum_scatter(delta_parts, "group", scatter_dimension=0, tiled=True).reshape(
        queries_dev, emb_width
    )
    code_terms = None
    for g in range(groups):
        term = jnp.dot(grad[g].T, q_all[g], preferred_element_type=jnp.float32)
        term = jnp.where(g == group_index, term, term.astype(jnp.bfloat16).astype(jnp.float32))
        code_terms = term if code_terms is None else code_terms + term
    code_delta = lax.psum_scatter(
        code_terms.astype(jnp.bfloat16), "member", scatter_dimension=0, tiled=True
    ).astype(jnp.float32)
    dz_query = norm_back(query_delta, q_unit, q_inv)
    dz_code = norm_back(code_delta, c_unit, c_inv)
    query_grad = jnp.einsum(
        "qe,de->qd", dz_query, projection, preferred_element_type=jnp.float32
    ).astype(jnp.bfloat16)
    code_grad = jnp.einsum(
        "qe,de->qd", dz_code, projection, preferred_element_type=jnp.float32
    ).astype(jnp.bfloat16)
    dz_all = lax.all_gather(jnp.stack([dz_query, dz_code], axis=0), "member", axis=0)
    proj_parts = jnp.einsum(
        "mtqgr,mtqe->gre", feat_cols, dz_all, preferred_element_type=jnp.float32
    )
    projection_grad = lax.psum_scatter(
        proj_parts, "group", scatter_dimension=0, tiled=True
    ).reshape(rows_dev, emb_width)
    return (query_grad, code_grad, projection_grad)


def solution(mesh):
    return jax.shard_map(
        body,
        mesh=mesh,
        in_specs=(
            P(("group", "member"), None),
            P(("group", "member"), None),
            P(),
            P(("group", "member"), None),
            P(("group", "member")),
        ),
        out_specs=(
            P(("group", "member"), None),
            P(("group", "member"), None),
            P(("group", "member"), None),
        ),
        check_vma=False,
    )
```

profile of v0, /device:TPU:0, one launch (start us, length us, event | category | flops | bytes accessed | tf_op | source)
XLA Modules:
  0.0 291.4 jit_solution(1036864795923591170)
XLA Ops:
  7.2 5.1 %multiply_reduce_fusion.1 = (f32[128]{0:T(128)S(1)}, f32[128,1024]{1,0:T(8,128)S(1)}) fusion(bf16[128,4096]{1,0:T(8,128)(2,1)} %param.5, bf16[4096,1024]{1,0:T(8,128)(2,1)} %param.7), kind=kOutput, calls=%fused_computation.25 | convolution fusion | flops 1074003840 | bytes 9961984 | tf_op jit(solution)/shard_map/dot_general | solution.py:12
  12.3 0.8 multiply_convert_fusion.2
  13.6 4.7 %multiply_reduce_fusion = (f32[128]{0:T(128)S(1)}, f32[128,1024]{1,0:T(8,128)S(1)}) fusion(bf16[128,4096]{1,0:T(8,128)(2,1)S(1)} %copy-done, bf16[4096,1024]{1,0:T(8,128)(2,1)} %param.7), kind=kOutput, calls=%fused_computation.24 | convolution fusion | flops 1074003840 | bytes 9961984 | tf_op jit(solution)/shard_map/dot_general | solution.py:12
  18.3 0.8 multiply_convert_fusion.1
  19.2 12.9 %all-gather.5 = s32[4,1,16]{2,1,0:T(1,128)S(1)} all-gather(s32[1,1,16]{2,1,0:T(1,128)S(1)} %bitcast.92), channel_id=1, replica_groups=mesh['group'=4,'member'=8] {'group'}, dimensions={0}, use_global_device_ids=true | all-gather | bytes 320 | tf_op jit(solution)/shard_map/all_gather | solution.py:44
  32.5 7.9 %all-gather.4 = f32[4,1,128]{2,1,0:T(1,128)S(1)} all-gather(f32[1,1,128]{2,1,0:T(1,128)S(1)} %bitcast.93), channel_id=2, replica_groups=mesh['group'=4,'member'=8] {'group'}, dimensions={0}, use_global_device_ids=true | all-gather | bytes 2560 | tf_op jit(solution)/shard_map/all_gather | solution.py:45
  40.4 0.9 fusion.12
  41.3 2.8 all-gather.12.cloned.1.call-done
  44.0 29.7 %all-gather.10.cloned.1.call-done = bf16[1024,1024]{1,0:T(8,128)(2,1)} async-done(((bf16[128,1024]{1,0:T(8,128)(2,1)}), bf16[1024,1024]{1,0:T(8,128)(2,1)}) %all-gather.10.cloned.1.call-update) | async-done | bytes 2097168 | tf_op jit(solution)/shard_map/all_gather | solution.py:42
  73.7 3.3 %fusion.24 = (f32[4,128]{1,0:T(4,128)S(1)}, f32[4,128,1024]{2,1,0:T(8,128)S(1)}) fusion(bf16[4,128,1024]{2,1,0:T(8,128)(2,1)} %bitcast.85, bf16[1024,1024]{1,0:T(8,128)(2,1)} %all-gather.10.cloned.1.call-done, pred[4,1024]{1,0:T(4,128)(4,1)S(1)} %broadcast_in_dim.21), kind=kOutput, calls=%fused_computation.58 | convolution fusion | flops 1075314176 | bytes 5249024 | tf_op jit(solution)/shard_map/gqe,ke->gqk/dot_general | solution.py:53
  77.5 13.4 %all-gather.2 = f32[8,4,128]{2,1,0:T(4,128)S(1)} all-gather(f32[2,4,128]{2,1,0:T(4,128)S(1)} %pad_maximum_fusion.1), channel_id=4, replica_groups=mesh['group'=4,'member'=8] {'group'}, dimensions={0}, use_global_device_ids=true | all-gather | bytes 20480 | tf_op jit(solution)/shard_map/all_gather | solution.py:60
  91.0 0.6 multiply_convert_fusion
  91.6 0.7 fusion.14
  92.3 0.7 fusion.16
  93.1 0.7 fusion.18
  93.8 2.4 add_convert_fusion
  96.3 4.1 %fusion = f32[4,128,1024]{2,1,0:T(8,128)} fusion(bf16[4,128,1024]{2,1,0:T(8,128)(2,1)S(1)} %multiply_convert_fusion, bf16[1024,1024]{1,0:T(8,128)(2,1)} %all-gather.10.cloned.1.call-done), kind=kOutput, calls=%fused_computation.4 | convolution fusion | flops 1073741824 | bytes 5242880 | tf_op jit(solution)/shard_map/gqk,ke->gqe/dot_general | solution.py:74
  100.5 37.0 %reduce-scatter.6.cloned.1.call-done = bf16[128,1024]{1,0:T(8,128)(2,1)} async-done(((bf16[1024,1024]{1,0:T(8,128)(2,1)}), bf16[128,1024]{1,0:T(8,128)(2,1)}) %reduce-scatter.6.cloned.1.call-update) | async-done | bytes 262160 | tf_op jit(solution)/shard_map/reduce_scatter | solution.py:83
  137.4 1.2 fusion.6
  138.6 1.1 fusion.8
  139.7 43.5 %reduce-scatter.4.cloned.1.call-done = f32[1,128,1024]{2,1,0:T(8,128)} async-done(((f32[4,128,1024]{2,1,0:T(8,128)}), f32[1,128,1024]{2,1,0:T(8,128)}) %reduce-scatter.4.cloned.1.call-update) | async-done | bytes 524304 | tf_op jit(solution)/shard_map/reduce_scatter | solution.py:75
  183.2 1.2 fusion.9
  184.5 1.2 fusion.11
  185.7 0.8 pad_maximum_fusion
  186.6 0.7 copy.19
  187.3 0.7 copy.18
  188.3 38.3 %all_to_all.5 = bf16[8,2,128,4,128]{2,4,1,3,0:T(8,128)(2,1)} all-to-all(bf16[8,2,128,4,128]{2,4,1,3,0:T(8,128)(2,1)S(1)} %copy.20), channel_id=1, replica_groups=mesh['group'=4,'member'=8] {'member'}, dimensions={0} | all-to-all | bytes 4194304 | tf_op jit(solution)/shard_map/all_to_all | solution.py:39
  226.6 9.4 %all-gather.14.cloned.1.call-done = bf16[16,128,1024]{2,1,0:T(8,128)(2,1)} async-done(((bf16[2,128,1024]{2,1,0:T(8,128)(2,1)}), bf16[16,128,1024]{2,1,0:T(8,128)(2,1)}) %all-gather.14.cloned.1.call-update) | async-done | bytes 4194320 | tf_op jit(solution)/shard_map/all_gather | solution.py:94
  236.0 6.5 %convolution_bitcast_fusion = f32[4,128,1024]{2,1,0:T(8,128)} fusion(bf16[8,2,128,4,128]{2,4,1,3,0:T(8,128)(2,1)} %all_to_all.5, bf16[8,2,128,1024,1]{3,2,1,4,0:T(8,128)(2,1)} %bitcast.94), kind=kOutput, calls=%fused_computation.11 | convolution fusion | flops 2147483648 | bytes 8388608 | tf_op jit(solution)/shard_map/mtqgr,mtqe->gre/dot_general | solution.py:95
  242.5 7.3 %convolution_convert_fusion = bf16[128,4096]{1,0:T(8,128)(2,1)} fusion(bf16[128,1024]{1,0:T(8,128)(2,1)S(1)} %fusion.8, bf16[4096,1024]{1,0:T(8,128)(2,1)} %param.7), kind=kOutput, calls=%fused_computation | convolution fusion | flops 1074266112 | bytes 9699328 | tf_op jit(solution)/shard_map/qe,de->qd/dot_general | solution.py:91
  249.8 7.2 %convolution_convert_fusion.1 = bf16[128,4096]{1,0:T(8,128)(2,1)} fusion(bf16[128,1024]{1,0:T(8,128)(2,1)S(1)} %copy-done.3, bf16[4096,1024]{1,0:T(8,128)(2,1)} %param.7), kind=kOutput, calls=%fused_computation.1 | convolution fusion | flops 1074266112 | bytes 9699328 | tf_op jit(solution)/shard_map/qe,de->qd/dot_general | solution.py:88
  257.0 27.5 %reduce-scatter.8.cloned.1.call-done = f32[1,128,1024]{2,1,0:T(8,128)} async-done(((f32[4,128,1024]{2,1,0:T(8,128)}), f32[1,128,1024]{2,1,0:T(8,128)}) %reduce-scatter.8.cloned.1.call-update) | async-done | bytes 524304 | tf_op jit(solution)/shard_map/reduce_scatter | solution.py:98
  (47 shorter events, 2.1 us)
Async XLA Ops:
  7.2 36.9 %all-gather.12.cloned.1.call-start = ((), (), s32[]{:S(2)}) async-start(), calls=%async_computation.8 | async-start | bytes 1310720 | tf_op jit(solution)/shard_map/all_gather | solution.py:43
  12.3 1.3 copy-start
  13.1 6.1 %copy-start.6 = (s32[1,16]{1,0:T(1,128)S(1)}, s32[1,16]{1,0:T(1,128)}, u32[]{:S(2)}) copy-start(s32[1,16]{1,0:T(1,128)} %param.8) | copy-start | bytes 196
  13.1 19.4 %copy-start.7 = (f32[128]{0:T(128)S(1)}, f32[128]{0:T(128)}, u32[]{:S(2)}) copy-start(f32[128]{0:T(128)} %param.9) | copy-start | bytes 1540
  13.1 60.5 %all-gather.10.cloned.1.call-start = ((), (), s32[]{:S(2)}) async-start(), calls=%async_computation.4 | async-start | bytes 2359296 | tf_op jit(solution)/shard_map/all_gather | solution.py:42
  19.2 118.3 %reduce-scatter.6.cloned.1.call-start = ((), (), s32[]{:S(2)}) async-start(), calls=%async_computation.6 | async-start | bytes 2359296 | tf_op jit(solution)/shard_map/reduce_scatter | solution.py:83
  77.0 14.0 %copy-start.4 = (f32[128,1024]{1,0:T(8,128)S(1)}, f32[128,1024]{1,0:T(8,128)}, u32[]{:S(2)}) copy-start(f32[128,1024]{1,0:T(8,128)} %fusion.12) | copy-start | bytes 1572868
  77.5 14.1 %copy-start.5 = (bf16[512,1024]{1,0:T(8,128)(2,1)S(1)}, bf16[512,1024]{1,0:T(8,128)(2,1)}, u32[]{:S(2)}) copy-start(bf16[512,1024]{1,0:T(8,128)(2,1)} %all-gather.12.cloned.1.call-done) | copy-start | bytes 3145732
  96.2 87.0 %reduce-scatter.4.cloned.1.call-start = ((), (), s32[]{:S(2)}) async-start(), calls=%async_computation.5 | async-start | bytes 2621440 | tf_op jit(solution)/shard_map/reduce_scatter | solution.py:75
  100.4 135.6 %all-gather.14.cloned.1.call-start = ((), (), s32[]{:S(2)}) async-start(), calls=%async_computation.9 | async-start | bytes 4718592 | tf_op jit(solution)/shard_map/all_gather | solution.py:94
  185.7 0.9 copy-start.2
  185.7 1.6 copy-start.1
  186.6 98.0 %reduce-scatter.8.cloned.1.call-start = ((), (), s32[]{:S(2)}) async-start(), calls=%async_computation.7 | async-start | bytes 2621440 | tf_op jit(solution)/shard_map/reduce_scatter | solution.py:98
  242.5 7.3 %copy-start.3 = (bf16[128,1024]{1,0:T(8,128)(2,1)S(1)}, bf16[128,1024]{1,0:T(8,128)(2,1)}, u32[]{:S(2)}) copy-start(bf16[128,1024]{1,0:T(8,128)(2,1)} %copy-done.2) | copy-start | bytes 786436
Sparse Core Ops, SparseCore 0:
  13.2 30.7 all-gather.11
  46.5 27.1 all-gather.9
  96.3 41.0 reduce-scatter.5
  139.6 43.5 reduce-scatter.3
  186.7 49.2 all-gather.13
  242.6 41.9 reduce-scatter.7
where the time goes:
time: 292 us; the launch traced here: 291 us
  waiting for transfers between devices  150 us (51%)
  blocking collectives  72.5 us (25%)
  matrix products  42.8 us (15%)
  between operations  14.3 us (5%)
  other arithmetic  9.61 us (3%)
    reduce_scatter x1, waiting for transfers between devices, body(): lax.psum_scatter(delta_parts, 'group', scatter_dimension=0, tiled=True)  43.5 us
    all_to_all x1, blocking collectives, body(): lax.all_to_all(feats, 'member', split_axis=0, concat_axis=0, tiled=True)  38.3 us
    reduce_scatter x1, waiting for transfers between devices, body(): lax.psum_scatter(code_terms.astype(jnp.bfloat16), 'member', scatter_dimen...  37 us
    all_gather x1, waiting for transfers between devices, body(): group_codes = lax.all_gather(c_emb, 'member', axis=0, tiled=True)  29.7 us
    reduce_scatter x1, waiting for transfers between devices, body(): lax.psum_scatter(proj_parts, 'group', scatter_dimension=0, tiled=True)  27.5 us
    all_gather x1, blocking collectives, body(): lax.all_gather(jnp.stack([part_max, part_sum], axis=0), 'group', axis=0)  13.4 us
    all_gather x1, blocking collectives, body(): ids_all = lax.all_gather(hard_ids[0], 'group', axis=0)  12.9 us
    dot_general x2, matrix products, embed(): values = jnp.dot(features, projection, preferred_element_type=jnp.float32)  9.78 us
  transfers between devices with their start and end apart: 6, of which 6 were waited for; matrix products, arithmetic and copies ran while one was open for 10% of the time, Pallas kernels for 0%

commit v1 on v0

--- a/solution.py
+++ b/solution.py
@@ -6,6 +6,23 @@
 CB = 64
 inverse_temp = 120.0
 epsilon = 1e-06
+
+
+def laid_out(tiles, dim):
+    lengths = list(tiles.shape[1:])
+    lengths[dim] *= tiles.shape[0]
+    return jnp.moveaxis(tiles, 0, dim).reshape(lengths)
+
+
+def ring_gather(x, axis, dim):
+    count = lax.axis_size(axis)
+    right = [(i, (i + 1) % count) for i in range(count)]
+    pieces = [x]
+    while len(pieces) < count:
+        pieces.append(lax.ppermute(pieces[-1], axis, right))
+    index = lax.axis_index(axis)
+    pieces = jnp.stack(pieces)[(index - jnp.arange(count)) % count]
+    return laid_out(pieces, dim)
 
 
 def embed(features, projection):
@@ -39,7 +56,7 @@
     feat_cols = lax.all_to_all(feats, "member", split_axis=0, concat_axis=0, tiled=True)
     q_unit, q_inv, q_emb = embed(query_feat, projection)
     c_unit, c_inv, c_emb = embed(code_feat, projection)
-    group_codes = lax.all_gather(c_emb, "member", axis=0, tiled=True)
+    group_codes = ring_gather(c_emb, "member", 0)
     q_all = lax.all_gather(q_emb, "group", axis=0)
     ids_all = lax.all_gather(hard_ids[0], "group", axis=0)
     w_all = lax.all_gather(loss_weight, "group", axis=0)

time: 292 us -> 295 us (1.010)
  local copies, waits for them, and re-layouts: 2.08 us -> 11.5 us
  waiting for transfers between devices: 150 us -> 144 us
    all_gather x1 -> x0, waiting for transfers between devices: 29.7 us -> none  [body(): group_codes = lax.all_gather(c_emb, 'member', axis=0, tiled=True)]
    ppermute x0 -> x7, waiting for transfers between devices: none -> 27.9 us  [ring_gather(): pieces.append(lax.ppermute(pieces[-1], axis, right))]
    unnamed x18 -> x24, local copies, waits for them, and re-layouts: 1.77 us -> 6.81 us
    gather x0 -> x1, local copies, waits for them, and re-layouts: none -> 3.62 us  [ring_gather(): pieces = jnp.stack(pieces)[(index - jnp.arange(count)) % count]]
  transfers between devices with their start and end apart: 6 -> 12, of which waited for: 6 -> 9; matrix products, arithmetic and copies ran while one was open for 10% -> 13% of each run, Pallas kernels for 0% -> 0%
where the time goes in v1:
time: 295 us
  waiting for transfers between devices  144 us (49%)
  blocking collectives  71.8 us (24%)
  matrix products  42.8 us (15%)
  between operations  14 us (5%)
  local copies, waits for them, and re-layouts  11.5 us (4%)
  other arithmetic  9.66 us (3%)
    reduce_scatter x1, waiting for transfers between devices, body(): lax.psum_scatter(delta_parts, 'group', scatter_dimension=0, tiled=True)  43.6 us
    all_to_all x1, blocking collectives, body(): lax.all_to_all(feats, 'member', split_axis=0, concat_axis=0, tiled=True)  38.3 us
    reduce_scatter x1, waiting for transfers between devices, body(): lax.psum_scatter(code_terms.astype(jnp.bfloat16), 'member', scatter_dimen...  35.6 us
    ppermute x7, waiting for transfers between devices, ring_gather(): pieces.append(lax.ppermute(pieces[-1], axis, right))  27.9 us
    reduce_scatter x1, waiting for transfers between devices, body(): lax.psum_scatter(proj_parts, 'group', scatter_dimension=0, tiled=True)  27.5 us
    all_gather x1, blocking collectives, body(): lax.all_gather(jnp.stack([part_max, part_sum], axis=0), 'group', axis=0)  13.3 us
    all_gather x1, blocking collectives, body(): ids_all = lax.all_gather(hard_ids[0], 'group', axis=0)  12.4 us
    dot_general x2, matrix products, embed(): values = jnp.dot(features, projection, preferred_element_type=jnp.float32)  9.78 us
  transfers between devices with their start and end apart: 12, of which 9 were waited for; matrix products, arithmetic and copies ran while one was open for 13% of the time, Pallas kernels for 0%

profile of v1, /device:TPU:0, one launch (start us, length us, event | category | flops | bytes accessed | tf_op | source)
XLA Modules:
  0.0 294.7 jit_solution(6427498882713667361)
XLA Ops:
  7.2 5.1 %multiply_reduce_fusion.1 = (f32[128]{0:T(128)S(1)}, f32[128,1024]{1,0:T(8,128)S(1)}) fusion(bf16[128,4096]{1,0:T(8,128)(2,1)} %param.5, bf16[4096,1024]{1,0:T(8,128)(2,1)} %param.7), kind=kOutput, calls=%fused_computation.22 | convolution fusion | flops 1074003840 | bytes 9961984 | tf_op jit(solution)/shard_map/dot_general | solution.py:29
  12.3 0.8 multiply_convert_fusion.2
  13.6 4.7 %multiply_reduce_fusion = (f32[128]{0:T(128)S(1)}, f32[128,1024]{1,0:T(8,128)S(1)}) fusion(bf16[128,4096]{1,0:T(8,128)(2,1)S(1)} %copy-done, bf16[4096,1024]{1,0:T(8,128)(2,1)} %param.7), kind=kOutput, calls=%fused_computation.21 | convolution fusion | flops 1074003840 | bytes 9961984 | tf_op jit(solution)/shard_map/dot_general | solution.py:29
  18.3 0.8 bitcast_dynamic-update-slice_fusion.7
  19.7 12.4 %all-gather.5 = s32[4,1,16]{2,1,0:T(1,128)S(1)} all-gather(s32[1,1,16]{2,1,0:T(1,128)S(1)} %bitcast.108), channel_id=1, replica_groups=mesh['group'=4,'member'=8] {'group'}, dimensions={0}, use_global_device_ids=true | all-gather | bytes 320 | tf_op jit(solution)/shard_map/all_gather | solution.py:61
  32.4 6.6 %collective-permute-done.1 = bf16[128,1024]{1,0:T(8,128)(2,1)S(1)} collective-permute-done((bf16[128,1024]{1,0:T(8,128)(2,1)S(1)}, bf16[128,1024]{1,0:T(8,128)(2,1)S(1)}, u32[]{:S(2)}, u32[]{:S(2)}) %collective-permute-start.1) | collective-permute-done | bytes 262176 | tf_op jit(solution)/shard_map/ppermute | solution.py:22
  39.0 7.7 %all-gather.4 = f32[4,1,128]{2,1,0:T(1,128)S(1)} all-gather(f32[1,1,128]{2,1,0:T(1,128)S(1)} %bitcast.109), channel_id=2, replica_groups=mesh['group'=4,'member'=8] {'group'}, dimensions={0}, use_global_device_ids=true | all-gather | bytes 2560 | tf_op jit(solution)/shard_map/all_gather | solution.py:62
  46.8 0.9 fusion.6
  47.7 5.6 %collective-permute-done.3 = bf16[128,1024]{1,0:T(8,128)(2,1)S(1)} collective-permute-done((bf16[128,1024]{1,0:T(8,128)(2,1)S(1)}, bf16[128,1024]{1,0:T(8,128)(2,1)S(1)}, u32[]{:S(2)}, u32[]{:S(2)}) %collective-permute-start.3) | collective-permute-done | bytes 262176 | tf_op jit(solution)/shard_map/ppermute | solution.py:22
  54.8 5.3 %collective-permute-done.4 = bf16[128,1024]{1,0:T(8,128)(2,1)S(1)} collective-permute-done((bf16[128,1024]{1,0:T(8,128)(2,1)S(1)}, bf16[128,1024]{1,0:T(8,128)(2,1)S(1)}, u32[]{:S(2)}, u32[]{:S(2)}) %collective-permute-start.4) | collective-permute-done | bytes 262176 | tf_op jit(solution)/shard_map/ppermute | solution.py:22
  61.5 5.2 %collective-permute-done.5 = bf16[128,1024]{1,0:T(8,128)(2,1)S(1)} collective-permute-done((bf16[128,1024]{1,0:T(8,128)(2,1)S(1)}, bf16[128,1024]{1,0:T(8,128)(2,1)S(1)}, u32[]{:S(2)}, u32[]{:S(2)}) %collective-permute-start.5) | collective-permute-done | bytes 262176 | tf_op jit(solution)/shard_map/ppermute | solution.py:22
  68.2 5.2 %collective-permute-done.6 = bf16[128,1024]{1,0:T(8,128)(2,1)S(1)} collective-permute-done((bf16[128,1024]{1,0:T(8,128)(2,1)S(1)}, bf16[128,1024]{1,0:T(8,128)(2,1)S(1)}, u32[]{:S(2)}, u32[]{:S(2)}) %collective-permute-start.6) | collective-permute-done | bytes 262176 | tf_op jit(solution)/shard_map/ppermute | solution.py:22
  74.2 3.6 %gather_fusion = bf16[8,128,1024]{2,1,0:T(8,128)(2,1)} fusion(bf16[8,128,1024]{2,1,0:T(8,128)(2,1)} %bitcast_dynamic-update-slice_fusion, s32[1024]{0:T(1024)S(1)} %pad_clamp_fusion), kind=kCustom, calls=%fused_computation | custom fusion | bytes 4194336 | tf_op jit(solution)/shard_map/gather | solution.py:24
  77.8 3.3 %fusion.20 = (f32[4,128]{1,0:T(4,128)S(1)}, f32[4,128,1024]{2,1,0:T(8,128)S(1)}) fusion(bf16[4,128,1024]{2,1,0:T(8,128)(2,1)} %bitcast.101, bf16[1024,1024,1]{1,0,2:T(8,128)(2,1)} %bitcast.99, pred[4,1024]{1,0:T(4,128)(4,1)S(1)} %broadcast_in_dim.21), kind=kOutput, calls=%fused_computation.70 | convolution fusion | flops 1075314176 | bytes 5249024 | tf_op jit(solution)/shard_map/gqe,ke->gqk/dot_general | solution.py:70
  81.6 13.3 %all-gather.2 = f32[8,4,128]{2,1,0:T(4,128)S(1)} all-gather(f32[2,4,128]{2,1,0:T(4,128)S(1)} %pad_maximum_fusion.1), channel_id=4, replica_groups=mesh['group'=4,'member'=8] {'group'}, dimensions={0}, use_global_device_ids=true | all-gather | bytes 20480 | tf_op jit(solution)/shard_map/all_gather | solution.py:77
  95.6 0.7 fusion.8
  97.1 0.7 fusion.12
  97.9 2.4 add_convert_fusion
  100.3 4.1 %fusion.21 = f32[4,128,1024]{2,1,0:T(8,128)} fusion(bf16[4,128,1024]{2,1,0:T(8,128)(2,1)S(1)} %multiply_convert_fusion, bf16[1024,1024,1]{1,0,2:T(8,128)(2,1)} %bitcast.100), kind=kOutput, calls=%fused_computation.71 | convolution fusion | flops 1073741824 | bytes 5242880 | tf_op jit(solution)/shard_map/gqk,ke->gqe/dot_general | solution.py:91
  104.5 35.6 %reduce-scatter.6.cloned.1.call-done = bf16[128,1024]{1,0:T(8,128)(2,1)} async-done(((bf16[1024,1024]{1,0:T(8,128)(2,1)}), bf16[128,1024]{1,0:T(8,128)(2,1)}) %reduce-scatter.6.cloned.1.call-update) | async-done | bytes 262160 | tf_op jit(solution)/shard_map/reduce_scatter | solution.py:100
  140.2 1.2 fusion
  141.4 1.1 fusion.2
  142.5 43.6 %reduce-scatter.4.cloned.1.call-done = f32[1,128,1024]{2,1,0:T(8,128)} async-done(((f32[4,128,1024]{2,1,0:T(8,128)}), f32[1,128,1024]{2,1,0:T(8,128)}) %reduce-scatter.4.cloned.1.call-update) | async-done | bytes 524304 | tf_op jit(solution)/shard_map/reduce_scatter | solution.py:92
  186.1 1.2 fusion.3
  187.4 1.2 fusion.5
  189.3 0.8 pad_maximum_fusion
  191.9 38.3 %all_to_all.5 = bf16[8,2,128,4,128]{2,4,1,3,0:T(8,128)(2,1)} all-to-all(bf16[8,2,128,4,128]{2,4,1,3,0:T(8,128)(2,1)S(1)} %copy.20), channel_id=1, replica_groups=mesh['group'=4,'member'=8] {'member'}, dimensions={0} | all-to-all | bytes 4194304 | tf_op jit(solution)/shard_map/all_to_all | solution.py:56
  230.2 9.3 %all-gather.11.cloned.1.call-done = bf16[16,128,1024]{2,1,0:T(8,128)(2,1)} async-done(((bf16[2,128,1024]{2,1,0:T(8,128)(2,1)}), bf16[16,128,1024]{2,1,0:T(8,128)(2,1)}) %all-gather.11.cloned.1.call-update) | async-done | bytes 4194320 | tf_op jit(solution)/shard_map/all_gather | solution.py:111
  239.6 6.5 %convolution_bitcast_fusion = f32[4,128,1024]{2,1,0:T(8,128)} fusion(bf16[8,2,128,4,128]{2,4,1,3,0:T(8,128)(2,1)} %all_to_all.5, bf16[8,2,128,1024,1]{3,2,1,4,0:T(8,128)(2,1)} %bitcast.110), kind=kOutput, calls=%fused_computation.8 | convolution fusion | flops 2147483648 | bytes 8388608 | tf_op jit(solution)/shard_map/mtqgr,mtqe->gre/dot_general | solution.py:112
  246.1 7.3 %convolution_convert_fusion = bf16[128,4096]{1,0:T(8,128)(2,1)} fusion(bf16[128,1024]{1,0:T(8,128)(2,1)S(1)} %fusion.2, bf16[4096,1024]{1,0:T(8,128)(2,1)} %param.7), kind=kOutput, calls=%fused_computation.1 | convolution fusion | flops 1074266112 | bytes 9699328 | tf_op jit(solution)/shard_map/qe,de->qd/dot_general | solution.py:108
  253.4 7.2 %convolution_convert_fusion.1 = bf16[128,4096]{1,0:T(8,128)(2,1)} fusion(bf16[128,1024]{1,0:T(8,128)(2,1)S(1)} %copy-done.3, bf16[4096,1024]{1,0:T(8,128)(2,1)} %param.7), kind=kOutput, calls=%fused_computation.2 | convolution fusion | flops 1074266112 | bytes 9699328 | tf_op jit(solution)/shard_map/qe,de->qd/dot_general | solution.py:105
  260.6 27.5 %reduce-scatter.8.cloned.1.call-done = f32[1,128,1024]{2,1,0:T(8,128)} async-done(((f32[4,128,1024]{2,1,0:T(8,128)}), f32[1,128,1024]{2,1,0:T(8,128)}) %reduce-scatter.8.cloned.1.call-update) | async-done | bytes 524304 | tf_op jit(solution)/shard_map/reduce_scatter | solution.py:115
  (68 shorter events, 11.0 us)
Async XLA Ops:
  7.2 70.6 %all-gather.9.cloned.1.call-start = ((), (), s32[]{:S(2)}) async-start(), calls=%async_computation.7 | async-start | bytes 1310720 | tf_op jit(solution)/shard_map/all_gather | solution.py:60
  12.3 1.3 copy-start
  13.1 6.6 %copy-start.6 = (s32[1,16]{1,0:T(1,128)S(1)}, s32[1,16]{1,0:T(1,128)}, u32[]{:S(2)}) copy-start(s32[1,16]{1,0:T(1,128)} %param.8) | copy-start | bytes 196
  13.1 25.9 %copy-start.7 = (f32[128]{0:T(128)S(1)}, f32[128]{0:T(128)}, u32[]{:S(2)}) copy-start(f32[128]{0:T(128)} %param.9) | copy-start | bytes 1540
  13.1 127.0 %reduce-scatter.6.cloned.1.call-start = ((), (), s32[]{:S(2)}) async-start(), calls=%async_computation.5 | async-start | bytes 2359296 | tf_op jit(solution)/shard_map/reduce_scatter | solution.py:100
  19.2 13.1 %collective-permute-start = (bf16[128,1024]{1,0:T(8,128)(2,1)S(1)}, bf16[128,1024]{1,0:T(8,128)(2,1)S(1)}, u32[]{:S(2)}, u32[]{:S(2)}) collective-permute-start(bf16[128,1024]{1,0:T(8,128)(2,1)S(1)} %get-tuple-element.4), channel_id=1, source_target_pairs={{0,1},{1,2},{2,3},{3,4},{4,5},{5,6},{6,7},{7,0},{8,9},{9,10},{10,1... | collective-permute-start | bytes 786440 | tf_op jit(solution)/shard_map/ppermute | solution.py:22
  32.2 6.7 %collective-permute-start.1 = (bf16[128,1024]{1,0:T(8,128)(2,1)S(1)}, bf16[128,1024]{1,0:T(8,128)(2,1)S(1)}, u32[]{:S(2)}, u32[]{:S(2)}) collective-permute-start(bf16[128,1024]{1,0:T(8,128)(2,1)S(1)} %collective-permute-done), channel_id=1, source_target_pairs={{0,1},{1,2},{2,3},{3,4},{4,5},{5,6},{6,7},{7,0},{8,9},{9,10},{10,1... | collective-permute-start | bytes 786440 | tf_op jit(solution)/shard_map/ppermute | solution.py:22
  39.0 7.7 %collective-permute-start.2 = (bf16[128,1024]{1,0:T(8,128)(2,1)S(1)}, bf16[128,1024]{1,0:T(8,128)(2,1)S(1)}, u32[]{:S(2)}, u32[]{:S(2)}) collective-permute-start(bf16[128,1024]{1,0:T(8,128)(2,1)S(1)} %collective-permute-done.1), channel_id=1, source_target_pairs={{0,1},{1,2},{2,3},{3,4},{4,5},{5,6},{6,7},{7,0},{8,9},{9,10},{10,1... | collective-permute-start | bytes 786440 | tf_op jit(solution)/shard_map/ppermute | solution.py:22
  46.6 6.7 %collective-permute-start.3 = (bf16[128,1024]{1,0:T(8,128)(2,1)S(1)}, bf16[128,1024]{1,0:T(8,128)(2,1)S(1)}, u32[]{:S(2)}, u32[]{:S(2)}) collective-permute-start(bf16[128,1024]{1,0:T(8,128)(2,1)S(1)} %collective-permute-done.2), channel_id=1, source_target_pairs={{0,1},{1,2},{2,3},{3,4},{4,5},{5,6},{6,7},{7,0},{8,9},{9,10},{10,1... | collective-permute-start | bytes 786440 | tf_op jit(solution)/shard_map/ppermute | solution.py:22
  53.3 6.7 %collective-permute-start.4 = (bf16[128,1024]{1,0:T(8,128)(2,1)S(1)}, bf16[128,1024]{1,0:T(8,128)(2,1)S(1)}, u32[]{:S(2)}, u32[]{:S(2)}) collective-permute-start(bf16[128,1024]{1,0:T(8,128)(2,1)S(1)} %collective-permute-done.3), channel_id=1, source_target_pairs={{0,1},{1,2},{2,3},{3,4},{4,5},{5,6},{6,7},{7,0},{8,9},{9,10},{10,1... | collective-permute-start | bytes 786440 | tf_op jit(solution)/shard_map/ppermute | solution.py:22
  60.0 6.7 %collective-permute-start.5 = (bf16[128,1024]{1,0:T(8,128)(2,1)S(1)}, bf16[128,1024]{1,0:T(8,128)(2,1)S(1)}, u32[]{:S(2)}, u32[]{:S(2)}) collective-permute-start(bf16[128,1024]{1,0:T(8,128)(2,1)S(1)} %collective-permute-done.4), channel_id=1, source_target_pairs={{0,1},{1,2},{2,3},{3,4},{4,5},{5,6},{6,7},{7,0},{8,9},{9,10},{10,1... | collective-permute-start | bytes 786440 | tf_op jit(solution)/shard_map/ppermute | solution.py:22
  66.7 6.7 %collective-permute-start.6 = (bf16[128,1024]{1,0:T(8,128)(2,1)S(1)}, bf16[128,1024]{1,0:T(8,128)(2,1)S(1)}, u32[]{:S(2)}, u32[]{:S(2)}) collective-permute-start(bf16[128,1024]{1,0:T(8,128)(2,1)S(1)} %collective-permute-done.5), channel_id=1, source_target_pairs={{0,1},{1,2},{2,3},{3,4},{4,5},{5,6},{6,7},{7,0},{8,9},{9,10},{10,1... | collective-permute-start | bytes 786440 | tf_op jit(solution)/shard_map/ppermute | solution.py:22
  81.1 14.0 %copy-start.4 = (f32[128,1024]{1,0:T(8,128)S(1)}, f32[128,1024]{1,0:T(8,128)}, u32[]{:S(2)}) copy-start(f32[128,1024]{1,0:T(8,128)} %fusion.6) | copy-start | bytes 1572868
  81.6 14.0 %copy-start.5 = (bf16[512,1024]{1,0:T(8,128)(2,1)S(1)}, bf16[512,1024]{1,0:T(8,128)(2,1)}, u32[]{:S(2)}) copy-start(bf16[512,1024]{1,0:T(8,128)(2,1)} %all-gather.9.cloned.1.call-done) | copy-start | bytes 3145732
  100.3 85.8 %reduce-scatter.4.cloned.1.call-start = ((), (), s32[]{:S(2)}) async-start(), calls=%async_computation.4 | async-start | bytes 2621440 | tf_op jit(solution)/shard_map/reduce_scatter | solution.py:92
  104.5 135.1 %all-gather.11.cloned.1.call-start = ((), (), s32[]{:S(2)}) async-start(), calls=%async_computation.8 | async-start | bytes 4718592 | tf_op jit(solution)/shard_map/all_gather | solution.py:111
  188.6 0.7 copy-start.2
  188.6 2.3 copy-start.1
  190.1 98.0 %reduce-scatter.8.cloned.1.call-start = ((), (), s32[]{:S(2)}) async-start(), calls=%async_computation.6 | async-start | bytes 2621440 | tf_op jit(solution)/shard_map/reduce_scatter | solution.py:115
  246.1 7.3 %copy-start.3 = (bf16[128,1024]{1,0:T(8,128)(2,1)S(1)}, bf16[128,1024]{1,0:T(8,128)(2,1)}, u32[]{:S(2)}) copy-start(bf16[128,1024]{1,0:T(8,128)(2,1)} %copy-done.2) | copy-start | bytes 786436
Sparse Core Ops, SparseCore 0:
  13.2 30.7 all-gather.8
  100.4 39.7 reduce-scatter.5
  142.5 43.5 reduce-scatter.3
  190.3 49.2 all-gather.10
  246.2 41.8 reduce-scatter.7
